TPU v7x, 32 devices: a whole 2x2x4 slice. The times are simulated.
32 devices in a mesh: section: 2 (over x), mp: 4 (over z), dp: 4 (over y, core).
Axes of the slice: x: 2, y: 2, z: 4, core: 2. Of those that a mesh axis runs over, the one named last changes fastest.
Arguments:
- text_in: bfloat16 [4, 2, 512, 8192], P('dp', 'section', None, 'mp'), may hold values from -6 to 6
- vision: bfloat16 [4, 2, 256, 8192], P('dp', 'section', None, 'mp'), may hold values from -6 to 6
- tile_counts: int32 [4, 2], P('dp'), may hold values from 1 to 4, as said below
- lengths: int32 [4, 2], P('dp', 'section'), may hold values from 128 to 512, as said below
- image_of: int32 [4, 2], P('dp'), may hold values from 0 to 1, each once within a row
- norm_gain: float32 [2, 8192], P('section'), may hold values from 0.5 to 1.5
- query_weight: bfloat16 [2, 8192, 4096], P('section', 'dp', 'mp'), may hold values from -0.0625 to 0.0625
- key_weight: bfloat16 [2, 8192, 1024], P('section', 'dp', 'mp'), may hold values from -0.0625 to 0.0625
- value_weight: bfloat16 [2, 8192, 1024], P('section', 'dp', 'mp'), may hold values from -0.0625 to 0.0625
- query_gain: float32 [2, 128], P('section')
- key_gain: float32 [2, 128], P('section')
- cross_gate: float32 [2], P('section'), may hold values from 0.4 to 1.5
- context_grad: bfloat16 [4, 2, 512, 4096], P('dp', 'section', None, 'mp'), may hold values from -6 to 6
Outputs:
- gated_context: bfloat16 [4, 2, 512, 4096], P('dp', 'section', None, 'mp')
- vision_grad: bfloat16 [4, 2, 256, 8192], P('dp', 'section', None, 'mp')
- key_weight_grad: bfloat16 [2, 8192, 1024], P('section', 'dp', 'mp')
- value_weight_grad: bfloat16 [2, 8192, 1024], P('section', 'dp', 'mp')
Inputs may be any that keep to these rules, and one draw needn't show every extreme that they name: `tile_counts`: some image has 4 tiles and some has one. `lengths`: some sample has the full 512 tokens. `image_of`: each row is a permutation of the sections.
All inputs are finite; a program needn't handle non-finite values.
Results may differ from a plain program's by a relative error of at most 0.018.
Values may be sent and summed in bfloat16 or wider, within the bound.
No kernel may reach another device: no remote copies, remote signals or barrier semaphores. Data moves between devices by JAX's collectives and lax.ppermute only.
A program may use at most 192 MiB of HBM per device.

v0:
```python
import jax
import jax.numpy as jnp
from jax import lax
from jax.sharding import PartitionSpec as P

HD = 128
TILE_ROWS = 64


def shifted(value, axis, steps):
    count = lax.axis_size(axis)
    pairs = [(source, (source + steps) % count) for source in range(count)]
    return lax.ppermute(value, axis, pairs)


def norm_rows(values, gain):
    values = values.astype(jnp.float32)
    scaled = values * lax.rsqrt(jnp.mean(values * values, axis=-1, keepdims=True) + 1e-05)
    return scaled * gain


def rounded(values):
    return lax.optimization_barrier(values.astype(jnp.bfloat16)).astype(jnp.float32)


def attend(queries, keys_raw, values_raw, key_norm, usable, present, gate_value):
    keys = rounded(norm_rows(keys_raw, key_norm))
    values = rounded(values_raw)
    text_rows, heads, depth = queries.shape
    groups = keys.shape[1]
    grouped = queries.astype(jnp.float32).reshape(text_rows, groups, heads // groups, depth)
    scores = jnp.einsum("tgjd,vgd->gjtv", grouped, keys) * depth ** (-0.5)
    scores = jnp.where(usable[None, None, None, :], scores, -1e30)
    highest = lax.stop_gradient(jnp.max(scores, axis=-1, keepdims=True))
    weights = jnp.exp(scores - highest)
    probs = rounded(weights / jnp.sum(weights, axis=-1, keepdims=True))
    context = jnp.einsum("gjtv,vgd->tgjd", probs, values).reshape(text_rows, heads * depth)
    return jnp.where(present[:, None], jnp.tanh(gate_value) * context, 0.0)


def per_device(
    text_in,
    vision,
    tile_counts,
    lengths,
    image_of,
    norm_gain,
    query_weight,
    key_weight,
    value_weight,
    query_gain,
    key_gain,
    cross_gate,
    context_grad,
):
    arrived = shifted(text_in, "section", 1)
    full_text = lax.all_gather(arrived, "mp", axis=3, tiled=True)[0, 0]
    text_rows = full_text.shape[0]
    normed = norm_rows(full_text, norm_gain[0]).astype(jnp.bfloat16)
    width_q = query_weight.shape[2]
    columns = normed
    query_raw = jnp.dot(
        columns,
        lax.all_gather(query_weight, "dp", axis=1, tiled=True)[0],
        preferred_element_type=jnp.float32,
    )
    queries = norm_rows(query_raw.reshape(text_rows, width_q // HD, HD), query_gain[0]).astype(
        jnp.bfloat16
    )
    key_full, value_full = (
        lax.all_gather(key_weight, "dp", axis=1, tiled=True),
        lax.all_gather(value_weight, "dp", axis=1, tiled=True),
    )
    key_full = key_full[0]
    value_full = value_full[0]
    slot_rows = vision.shape[2]
    part_width = vision.shape[3]
    wanted = image_of[0, lax.axis_index("section")]
    shard_piece = lax.all_gather(vision, "section", axis=1, tiled=True)
    owners = jnp.arange(shard_piece.shape[1])
    chosen = (owners == wanted)[:, None, None]
    taken = jnp.where(chosen, shard_piece[0], jnp.zeros_like(shard_piece[0]))
    image_part = jnp.sum(taken.astype(jnp.float32), axis=0).astype(jnp.bfloat16)
    image = lax.all_gather(image_part, "mp", axis=1, tiled=True)
    width_k = key_full.shape[1]
    keys_raw = jnp.dot(image, key_full, preferred_element_type=jnp.float32).reshape(
        slot_rows, width_k // HD, HD
    )
    values_raw = jnp.dot(image, value_full, preferred_element_type=jnp.float32).reshape(
        slot_rows, width_k // HD, HD
    )
    usable = jnp.arange(slot_rows) < tile_counts[0, wanted] * TILE_ROWS
    present = jnp.arange(text_rows) < lengths[0, 0]

    def forward(keys_in, values_in):
        return attend(queries, keys_in, values_in, key_gain[0], usable, present, cross_gate[0])

    context, pullback = jax.vjp(forward, keys_raw, values_raw)
    gated_context = context.astype(jnp.bfloat16).reshape(1, 1, text_rows, width_q)
    key_back, value_back = pullback(context_grad[0, 0].astype(jnp.float32))
    key_flat = key_back.reshape(slot_rows, width_k).astype(jnp.bfloat16)
    value_flat = value_back.reshape(slot_rows, width_k).astype(jnp.bfloat16)
    contract = (((1,), (1,)), ((), ()))
    partial_sum = lax.dot_general(key_flat, key_full, contract, preferred_element_type=jnp.float32)
    partial_sum = partial_sum + lax.dot_general(
        value_flat, value_full, contract, preferred_element_type=jnp.float32
    )
    partial_bf = partial_sum.astype(jnp.bfloat16)
    summed = lax.psum_scatter(
        partial_bf.astype(jnp.float32).astype(jnp.bfloat16), "mp", scatter_dimension=1, tiled=True
    )
    row_ids = jnp.arange(slot_rows * lax.axis_size("section"))
    taken = jnp.take(summed, row_ids % slot_rows, axis=0).astype(jnp.float32)
    routed = lax.psum_scatter(
        jnp.where((row_ids // slot_rows == wanted)[:, None], taken, 0.0).astype(jnp.bfloat16),
        "section",
        scatter_dimension=0,
        tiled=True,
    )
    vision_grad = routed.reshape(1, 1, slot_rows, part_width)
    columns = image
    inner = (((0,), (0,)), ((), ()))
    key_part = lax.dot_general(columns, key_flat, inner, preferred_element_type=jnp.float32).astype(
        jnp.bfloat16
    )
    value_part = lax.dot_general(
        columns, value_flat, inner, preferred_element_type=jnp.float32
    ).astype(jnp.bfloat16)
    both_grads = lax.psum_scatter(
        jnp.concatenate([key_part, value_part], axis=1).astype(jnp.float32).astype(jnp.bfloat16),
        "dp",
        scatter_dimension=0,
        tiled=True,
    )
    key_weight_grad = both_grads[:, :width_k][None]
    value_weight_grad = both_grads[:, width_k:][None]
    return (gated_context, vision_grad, key_weight_grad, value_weight_grad)


def solution(mesh):
    return jax.shard_map(
        per_device,
        mesh=mesh,
        in_specs=(
            P("dp", "section", None, "mp"),
            P("dp", "section", None, "mp"),
            P("dp", None),
            P("dp", "section"),
            P("dp", None),
            P("section", None),
            P("section", "dp", "mp"),
            P("section", "dp", "mp"),
            P("section", "dp", "mp"),
            P("section", None),
            P("section", None),
            P("section"),
            P("dp", "section", None, "mp"),
        ),
        out_specs=(
            P("dp", "section", None, "mp"),
            P("dp", "section", None, "mp"),
            P("section", "dp", "mp"),
            P("section", "dp", "mp"),
        ),
        check_vma=False,
    )
```

profile of v0, /device:TPU:0, one launch (start us, length us, event | category | flops | bytes accessed | tf_op | source)
XLA Modules:
  0.0 705.0 jit_solution(10474390815657424555)
XLA Ops:
  10.7 34.7 %all-gather.7.cloned.1.call-done = bf16[1,2,256,2048]{3,2,0,1:T(8,128)(2,1)} async-done(((bf16[1,1,256,2048]{3,2,0,1:T(8,128)(2,1)}), bf16[1,2,256,2048]{3,2,0,1:T(8,128)(2,1)}) %all-gather.7.cloned.1.call-update) | async-done | bytes 2097168 | tf_op jit(solution)/shard_map/all_gather | solution.py:79
  45.4 3.4 fusion.34
  49.3 47.3 %collective-permute-done = bf16[1,1,512,2048]{3,2,1,0:T(8,128)(2,1)S(1)} collective-permute-done((bf16[1,1,512,2048]{3,2,1,0:T(8,128)(2,1)}, bf16[1,1,512,2048]{3,2,1,0:T(8,128)(2,1)S(1)}, u32[]{:S(2)}, u32[]{:S(2)}) %collective-permute-start) | collective-permute-done | bytes 2097184 | tf_op jit(solution)/shard_map/ppermute | solution.py:13
  104.2 6.4 copy.51
  110.6 7.0 all-gather.11.cloned.1.call-done
  117.6 6.4 copy.50
  123.9 76.4 %all-gather.9.cloned.1.call-done = bf16[256,8192]{1,0:T(8,128)(2,1)} async-done(((bf16[256,2048]{1,0:T(8,128)(2,1)}), bf16[256,8192]{1,0:T(8,128)(2,1)}) %all-gather.9.cloned.1.call-update) | async-done | bytes 4194320 | tf_op jit(solution)/shard_map/all_gather | solution.py:84
  200.4 4.9 multiply_reduce_fusion.2
  209.6 140.3 %all-gather.15.cloned.1.call-done = bf16[1,1,512,8192]{3,2,1,0:T(8,128)(2,1)} async-done(((bf16[1,1,512,2048]{3,2,1,0:T(8,128)(2,1)}), bf16[1,1,512,8192]{3,2,1,0:T(8,128)(2,1)}) %all-gather.15.cloned.1.call-update) | async-done | bytes 8388624 | tf_op jit(solution)/shard_map/all_gather | solution.py:57
  350.0 5.1 fusion.1
  355.1 100.4 %all-gather.17.cloned.1.call-done = bf16[1,8192,1024]{2,1,0:T(8,128)(2,1)} async-done(((bf16[1,2048,1024]{2,1,0:T(8,128)(2,1)}), bf16[1,8192,1024]{2,1,0:T(8,128)(2,1)}) %all-gather.17.cloned.1.call-update) | async-done | bytes 16777232 | tf_op jit(solution)/shard_map/all_gather | solution.py:64
  455.5 21.4 %copy.52 = bf16[1024,8192]{1,0:T(8,128)(2,1)} copy(bf16[1024,8192]{0,1:T(8,128)(2,1)} %bitcast.150) | data formatting | bytes 33554432 | tf_op jit(solution)/shard_map/dot_general | solution.py:62
  477.0 14.8 %multiply_reduce_fusion = (f32[512,8]{0,1:T(8,128)S(1)}, f32[512,8,128]{0,2,1:T(8,128)S(1)}) fusion(bf16[8,128,8192]{2,1,0:T(8,128)(2,1)} %bitcast.151, bf16[1,1,512,8192]{3,2,1,0:T(8,128)(2,1)} %all-gather.15.cloned.1.call-done, f32[8192]{0:T(1024)S(1)} %bitcast.169, f32[512]{0:T(512)S(1)} %add_rsqrt_fusion.1), kind=kOutput, calls=%fused_computation.55 | convolution fusion | flops 8607756288 | bytes 27314176 | tf_op jit(solution)/shard_map/dot_general | solution.py:62
  492.3 5.1 fusion.101
  498.1 3.9 fusion.16
  508.4 3.4 fusion.4
  511.9 5.5 convolution_convert_fusion
  517.4 3.2 convolution_convert_fusion.1
  520.6 7.7 %pad_maximum_fusion = bf16[8192,512]{0,1:T(8,128)(2,1)} fusion(bf16[8192,256]{0,1:T(8,128)(2,1)} %convolution_convert_fusion, bf16[8192,256]{0,1:T(8,128)(2,1)} %convolution_convert_fusion.1), kind=kLoop, calls=%fused_computation.13 | loop fusion | flops 16777216 | bytes 16777216 | tf_op jit(solution)/shard_map/concatenate | solution.py:130
  529.1 59.6 %reduce-scatter.4.cloned.1.call-done = bf16[256,2048]{1,0:T(8,128)(2,1)} async-done(((bf16[256,8192]{1,0:T(8,128)(2,1)}), bf16[256,2048]{1,0:T(8,128)(2,1)}) %reduce-scatter.4.cloned.1.call-update) | async-done | bytes 1048592 | tf_op jit(solution)/shard_map/reduce_scatter | solution.py:109
  588.7 6.8 gather_fusion
  595.5 3.7 select_convert_fusion
  601.6 62.2 %reduce-scatter.8.cloned.1.call-done = bf16[2048,512]{0,1:T(8,128)(2,1)} async-done(((bf16[8192,512]{0,1:T(8,128)(2,1)}), bf16[2048,512]{0,1:T(8,128)(2,1)}) %reduce-scatter.8.cloned.1.call-update) | async-done | bytes 2097168 | tf_op jit(solution)/shard_map/reduce_scatter | solution.py:129
  668.0 30.4 %reduce-scatter.6.cloned.1.call-done = bf16[256,2048]{1,0:T(8,128)(2,1)} async-done(((bf16[512,2048]{1,0:T(8,128)(2,1)}), bf16[256,2048]{1,0:T(8,128)(2,1)}) %reduce-scatter.6.cloned.1.call-update) | async-done | bytes 1048592 | tf_op jit(solution)/shard_map/reduce_scatter | solution.py:114
  (89 shorter events, 27.4 us)
Async XLA Ops:
  7.2 38.2 %all-gather.7.cloned.1.call-start = ((), (), s32[]{:S(2)}) async-start(), calls=%async_computation.3 | async-start | bytes 3145728 | tf_op jit(solution)/shard_map/all_gather | solution.py:79
  7.9 96.3 %all-gather.13.cloned.1.call-start = ((), (), s32[]{:S(2)}) async-start(), calls=%async_computation.6 | async-start | bytes 5242880 | tf_op jit(solution)/shard_map/all_gather | solution.py:71
  8.7 108.9 %all-gather.11.cloned.1.call-start = ((), (), s32[]{:S(2)}) async-start(), calls=%async_computation.5 | async-start | bytes 5242880 | tf_op jit(solution)/shard_map/all_gather | solution.py:72
  9.4 191.0 %all-gather.9.cloned.1.call-start = ((), (), s32[]{:S(2)}) async-start(), calls=%async_computation.4 | async-start | bytes 5242880 | tf_op jit(solution)/shard_map/all_gather | solution.py:84
  48.8 51.1 %copy-start.12 = (bf16[1,1,512,1024]{3,2,1,0:T(8,128)(2,1)S(1)}, bf16[1,1,512,1024]{3,2,1,0:T(8,128)(2,1)}, u32[]{:S(2)}) copy-start(bf16[1,1,512,1024]{3,2,1,0:T(8,128)(2,1)} %param.25) | copy-start | bytes 3145732
  48.8 301.2 %all-gather.15.cloned.1.call-start = ((), (), s32[]{:S(2)}) async-start(), calls=%async_computation.7 | async-start | bytes 10485760 | tf_op jit(solution)/shard_map/all_gather | solution.py:57
  48.9 47.6 %collective-permute-start = (bf16[1,1,512,2048]{3,2,1,0:T(8,128)(2,1)}, bf16[1,1,512,2048]{3,2,1,0:T(8,128)(2,1)S(1)}, u32[]{:S(2)}, u32[]{:S(2)}) collective-permute-start(bf16[1,1,512,2048]{3,2,1,0:T(8,128)(2,1)} %param.13), channel_id=1, source_target_pairs={{0,16},{16,0},{1,17},{17,1},{2,18},{18,2},{3,19},{19,3},{4,20},{20... | collective-permute-start | bytes 6291464 | tf_op jit(solution)/shard_map/ppermute | solution.py:13
  97.9 4.5 copy-start.17
  98.0 357.6 %all-gather.17.cloned.1.call-start = ((), (), s32[]{:S(2)}) async-start(), calls=%async_computation.8 | async-start | bytes 20971520 | tf_op jit(solution)/shard_map/all_gather | solution.py:64
  98.5 490.2 %reduce-scatter.4.cloned.1.call-start = ((), (), s32[]{:S(2)}) async-start(), calls=%async_computation.9 | async-start | bytes 5242880 | tf_op jit(solution)/shard_map/reduce_scatter | solution.py:109
  200.4 4.9 copy-start.14
  200.4 5.7 copy-start.5
  200.4 5.9 copy-start.10
  455.5 21.4 %copy-start.16 = (f32[1,8192]{1,0:T(1,128)S(1)}, f32[1,8192]{1,0:T(1,128)}, u32[]{:S(2)}) copy-start(f32[1,8192]{1,0:T(1,128)} %param.18) | copy-start | bytes 98308
  477.0 14.8 %copy-start.15 = (f32[1,128]{1,0:T(1,128)S(1)}, f32[1,128]{1,0:T(1,128)}, u32[]{:S(2)}) copy-start(f32[1,128]{1,0:T(1,128)} %param.22) | copy-start | bytes 1540
  498.1 3.9 copy-start.8
  498.1 4.7 copy-start.9
  498.1 4.7 copy-start.13
  498.1 4.7 copy-start.18
  511.8 151.9 %reduce-scatter.8.cloned.1.call-start = ((), (), s32[]{:S(2)}) async-start(), calls=%async_computation.11 | async-start | bytes 10485760 | tf_op jit(solution)/shard_map/reduce_scatter | solution.py:129
  511.9 5.5 copy-start.6
  528.3 170.1 %reduce-scatter.6.cloned.1.call-start = ((), (), s32[]{:S(2)}) async-start(), calls=%async_computation.10 | async-start | bytes 3145728 | tf_op jit(solution)/shard_map/reduce_scatter | solution.py:114
  595.5 3.7 copy-start.3
  600.3 98.1 %copy-start.1 = (s32[1,2]{1,0:T(1,128)S(1)}, s32[1,2]{1,0:T(1,128)}, u32[]{:S(2)}) copy-start(s32[1,2]{1,0:T(1,128)} %param.17) | copy-start | bytes 28
  (5 other events, 10.3 us)
Sparse Core Ops, SparseCore 0:
  9.6 35.7 all-gather.6
  47.0 34.4 all-gather.12
  83.1 34.4 all-gather.10
  119.6 80.7 all-gather.8
  201.8 148.1 all-gather.14
  351.4 104.1 all-gather.16
  511.9 76.7 reduce-scatter.3
  591.5 72.2 reduce-scatter.7
  666.6 31.8 reduce-scatter.5
where the time goes:
time: 706 us; the launch traced here: 705 us
  waiting for transfers between devices  561 us (79%)
  local copies, waits for them, and re-layouts  51.3 us (7%)
  matrix products  44.1 us (6%)
  other arithmetic  30.3 us (4%)
  between operations  17.4 us (2%)
    all_gather x1, waiting for transfers between devices, per_device(): full_text = lax.all_gather(arrived, 'mp', axis=3, tiled=True)[0, 0]  140 us
    all_gather x1, waiting for transfers between devices, per_device(): lax.all_gather(query_weight, 'dp', axis=1, tiled=True)[0]  100 us
    all_gather x1, waiting for transfers between devices, per_device(): image = lax.all_gather(image_part, 'mp', axis=1, tiled=True)  76.4 us
    reduce_scatter x1, waiting for transfers between devices, per_device(): lax.psum_scatter(jnp.concatenate([key_part, value_part], axis=1).astype(j...  62.2 us
    reduce_scatter x1, waiting for transfers between devices, per_device(): lax.psum_scatter(partial_bf.astype(jnp.float32).astype(jnp.bfloat16), 'mp...  59.6 us
    ppermute x1, waiting for transfers between devices, shifted(): return lax.ppermute(value, axis, pairs)  47.3 us
    all_gather x1, waiting for transfers between devices, per_device(): shard_piece = lax.all_gather(vision, 'section', axis=1, tiled=True)  34.7 us
    reduce_scatter x1, waiting for transfers between devices, per_device(): lax.psum_scatter(jnp.where((row_ids // slot_rows == wanted)[:, None], tak...  30.4 us
  transfers between devices with their start and end apart: 10, of which 9 were waited for; matrix products, arithmetic and copies ran while one was open for 10% of the time, Pallas kernels for 0%

commit v1 on v0

--- a/solution.py
+++ b/solution.py
@@ -5,6 +5,12 @@
 
 HD = 128
 TILE_ROWS = 64
+
+
+def laid_out(blocks, dim):
+    shape = list(blocks.shape[1:])
+    shape[dim] *= blocks.shape[0]
+    return jnp.moveaxis(blocks, 0, dim).reshape(shape)
 
 
 def shifted(value, axis, steps):
@@ -81,7 +87,14 @@
     chosen = (owners == wanted)[:, None, None]
     taken = jnp.where(chosen, shard_piece[0], jnp.zeros_like(shard_piece[0]))
     image_part = jnp.sum(taken.astype(jnp.float32), axis=0).astype(jnp.bfloat16)
-    image = lax.all_gather(image_part, "mp", axis=1, tiled=True)
+    count_2 = lax.axis_size("mp")
+    ahead = [(i, (i + 1) % count_2) for i in range(count_2)]
+    tiles = [image_part]
+    while len(tiles) < count_2:
+        tiles.append(lax.ppermute(tiles[-1], "mp", ahead))
+    index = lax.axis_index("mp")
+    tiles = jnp.stack(tiles)[(index - jnp.arange(count_2)) % count_2]
+    image = laid_out(tiles, 1)
     width_k = key_full.shape[1]
     keys_raw = jnp.dot(image, key_full, preferred_element_type=jnp.float32).reshape(
         slot_rows, width_k // HD, HD

time: 706 us -> 656 us (0.929)
  waiting for transfers between devices: 561 us -> 487 us
  local copies, waits for them, and re-layouts: 51.3 us -> 64.2 us
    ppermute x0 -> x3, waiting for transfers between devices: none -> 79.1 us  [per_device(): tiles.append(lax.ppermute(tiles[-1], 'mp', ahead))]
    all_gather x1 -> x0, waiting for transfers between devices: 76.4 us -> none  [per_device(): image = lax.all_gather(image_part, 'mp', axis=1, tiled=True)]
    all_gather x1, waiting for transfers between devices: 140 us -> 84 us  [per_device(): full_text = lax.all_gather(arrived, 'mp', axis=3, tiled=True)[0, 0]]
    all_gather x1, waiting for transfers between devices: 34.7 us -> 0.02 us  [per_device(): shard_piece = lax.all_gather(vision, 'section', axis=1, tiled=True)]
    ppermute x1, waiting for transfers between devices: 47.3 us -> 68.3 us  [shifted(): return lax.ppermute(value, axis, pairs)]
  transfers between devices with their start and end apart: 10 -> 12, of which waited for: 9 -> 9; matrix products, arithmetic and copies ran while one was open for 10% -> 13% of each run, Pallas kernels for 0% -> 0%
where the time goes in v1:
time: 656 us; the launch traced here: 654 us
  waiting for transfers between devices  487 us (74%)
  local copies, waits for them, and re-layouts  64.2 us (10%)
  matrix products  47.6 us (7%)
  other arithmetic  33 us (5%)
  between operations  17.8 us (3%)
    all_gather x1, waiting for transfers between devices, per_device(): lax.all_gather(query_weight, 'dp', axis=1, tiled=True)[0]  100 us
    all_gather x1, waiting for transfers between devices, per_device(): full_text = lax.all_gather(arrived, 'mp', axis=3, tiled=True)[0, 0]  84 us
    ppermute x3, waiting for transfers between devices, per_device(): tiles.append(lax.ppermute(tiles[-1], 'mp', ahead))  79.1 us
    ppermute x1, waiting for transfers between devices, shifted(): return lax.ppermute(value, axis, pairs)  68.3 us
    reduce_scatter x1, waiting for transfers between devices, per_device(): lax.psum_scatter(jnp.concatenate([key_part, value_part], axis=1).astype(j...  62.2 us
    reduce_scatter x1, waiting for transfers between devices, per_device(): lax.psum_scatter(partial_bf.astype(jnp.float32).astype(jnp.bfloat16), 'mp...  59.6 us
    reduce_scatter x1, waiting for transfers between devices, per_device(): lax.psum_scatter(jnp.where((row_ids // slot_rows == wanted)[:, None], tak...  30.4 us
    dot_general x1, local copies, waits for them, and re-layouts, per_device(): jnp.dot(columns, lax.all_gather(query_weight, 'dp', axis=1, tiled=True)[0...  21.4 us
  transfers between devices with their start and end apart: 12, of which 9 were waited for; matrix products, arithmetic and copies ran while one was open for 13% of the time, Pallas kernels for 0%

profile of v1, /device:TPU:0, one launch (start us, length us, event | category | flops | bytes accessed | tf_op | source)
XLA Modules:
  0.0 654.3 jit_solution(1845855658397188529)
XLA Ops:
  12.4 68.3 %collective-permute-done.3 = bf16[1,1,512,2048]{3,2,1,0:T(8,128)(2,1)S(1)} collective-permute-done((bf16[1,1,512,2048]{3,2,1,0:T(8,128)(2,1)}, bf16[1,1,512,2048]{3,2,1,0:T(8,128)(2,1)S(1)}, u32[]{:S(2)}, u32[]{:S(2)}) %collective-permute-start.3) | collective-permute-done | bytes 2097184 | tf_op jit(solution)/shard_map/ppermute | solution.py:19
  88.4 24.3 %collective-permute-done = bf16[256,2048]{1,0:T(8,128)(2,1)S(1)} collective-permute-done((bf16[256,2048]{1,0:T(8,128)(2,1)S(1)}, bf16[256,2048]{1,0:T(8,128)(2,1)S(1)}, u32[]{:S(2)}, u32[]{:S(2)}) %collective-permute-start) | collective-permute-done | bytes 1048608 | tf_op jit(solution)/shard_map/ppermute | solution.py:94
  113.7 25.3 %collective-permute-done.1 = bf16[256,2048]{1,0:T(8,128)(2,1)} collective-permute-done((bf16[256,2048]{1,0:T(8,128)(2,1)S(1)}, bf16[256,2048]{1,0:T(8,128)(2,1)}, u32[]{:S(2)}, u32[]{:S(2)}) %collective-permute-start.1) | collective-permute-done | bytes 1048608 | tf_op jit(solution)/shard_map/ppermute | solution.py:94
  145.6 29.5 %collective-permute-done.2 = bf16[256,2048]{1,0:T(8,128)(2,1)} collective-permute-done((bf16[256,2048]{1,0:T(8,128)(2,1)}, bf16[256,2048]{1,0:T(8,128)(2,1)}, u32[]{:S(2)}, u32[]{:S(2)}) %collective-permute-start.2) | collective-permute-done | bytes 1048608 | tf_op jit(solution)/shard_map/ppermute | solution.py:94
  178.7 5.0 gather_fusion
  183.7 6.3 copy.69
  189.9 6.4 copy.72
  196.3 4.8 multiply_reduce_fusion.2
  201.9 6.4 copy.70
  208.3 4.8 convolution_convert_fusion.2
  215.1 84.0 %all-gather.12.cloned.1.call-done = bf16[1,1,512,8192]{3,2,1,0:T(8,128)(2,1)} async-done(((bf16[1,1,512,2048]{3,2,1,0:T(8,128)(2,1)}), bf16[1,1,512,8192]{3,2,1,0:T(8,128)(2,1)}) %all-gather.12.cloned.1.call-update) | async-done | bytes 8388624 | tf_op jit(solution)/shard_map/all_gather | solution.py:63
  299.2 5.1 fusion.1
  304.3 100.4 %all-gather.14.cloned.1.call-done = bf16[1,8192,1024]{2,1,0:T(8,128)(2,1)} async-done(((bf16[1,2048,1024]{2,1,0:T(8,128)(2,1)}), bf16[1,8192,1024]{2,1,0:T(8,128)(2,1)}) %all-gather.14.cloned.1.call-update) | async-done | bytes 16777232 | tf_op jit(solution)/shard_map/all_gather | solution.py:70
  404.6 21.4 %copy.74 = bf16[1024,8192]{1,0:T(8,128)(2,1)} copy(bf16[1024,8192]{0,1:T(8,128)(2,1)} %bitcast.158) | data formatting | bytes 33554432 | tf_op jit(solution)/shard_map/dot_general | solution.py:68
  426.1 14.8 %multiply_reduce_fusion = (f32[512,8]{0,1:T(8,128)S(1)}, f32[512,8,128]{0,2,1:T(8,128)S(1)}) fusion(bf16[8,128,8192]{2,1,0:T(8,128)(2,1)} %bitcast.159, bf16[1,1,512,8192]{3,2,1,0:T(8,128)(2,1)} %all-gather.12.cloned.1.call-done, f32[8192]{0:T(1024)S(1)} %bitcast.180, f32[512]{0:T(512)S(1)} %add_rsqrt_fusion.1), kind=kOutput, calls=%fused_computation.53 | convolution fusion | flops 8607756288 | bytes 27314176 | tf_op jit(solution)/shard_map/dot_general | solution.py:68
  441.4 5.1 fusion.96
  447.2 3.9 fusion.16
  460.9 5.6 convolution_convert_fusion
  469.8 7.7 %pad_maximum_fusion = bf16[8192,512]{0,1:T(8,128)(2,1)} fusion(bf16[8192,256]{0,1:T(8,128)(2,1)} %convolution_convert_fusion, bf16[8192,256]{0,1:T(8,128)(2,1)} %convolution_convert_fusion.1), kind=kLoop, calls=%fused_computation.14 | loop fusion | flops 16777216 | bytes 16777216 | tf_op jit(solution)/shard_map/concatenate | solution.py:143
  478.2 59.6 %reduce-scatter.4.cloned.1.call-done = bf16[256,2048]{1,0:T(8,128)(2,1)} async-done(((bf16[256,8192]{1,0:T(8,128)(2,1)}), bf16[256,2048]{1,0:T(8,128)(2,1)}) %reduce-scatter.4.cloned.1.call-update) | async-done | bytes 1048592 | tf_op jit(solution)/shard_map/reduce_scatter | solution.py:122
  537.8 6.8 %gather_fusion.1 = bf16[512,2048]{1,0:T(8,128)(2,1)} fusion(bf16[256,2048]{1,0:T(8,128)(2,1)} %reduce-scatter.4.cloned.1.call-done, s32[1024]{0:T(1024)S(1)} %pad_clamp_fusion), kind=kCustom, calls=%fused_computation.1 | custom fusion | bytes 4196352 | tf_op jit(solution)/shard_map/jit(_take)/gather | solution.py:126
  544.6 3.7 select_convert_fusion
  550.6 62.2 %reduce-scatter.8.cloned.1.call-done = bf16[2048,512]{0,1:T(8,128)(2,1)} async-done(((bf16[8192,512]{0,1:T(8,128)(2,1)}), bf16[2048,512]{0,1:T(8,128)(2,1)}) %reduce-scatter.8.cloned.1.call-update) | async-done | bytes 2097168 | tf_op jit(solution)/shard_map/reduce_scatter | solution.py:142
  617.1 30.4 %reduce-scatter.6.cloned.1.call-done = bf16[256,2048]{1,0:T(8,128)(2,1)} async-done(((bf16[512,2048]{1,0:T(8,128)(2,1)}), bf16[256,2048]{1,0:T(8,128)(2,1)}) %reduce-scatter.6.cloned.1.call-update) | async-done | bytes 1048592 | tf_op jit(solution)/shard_map/reduce_scatter | solution.py:127
  (93 shorter events, 45.0 us)
Async XLA Ops:
  7.2 75.7 %copy-start = (s32[1,2]{1,0:T(1,128)S(1)}, s32[1,2]{1,0:T(1,128)}, u32[]{:S(2)}) copy-start(s32[1,2]{1,0:T(1,128)} %param.17) | copy-start | bytes 28
  7.2 76.9 %all-gather.6.cloned.1.call-start = ((), (), s32[]{:S(2)}) async-start(), calls=%async_computation.3 | async-start | bytes 3145728 | tf_op jit(solution)/shard_map/all_gather | solution.py:85
  7.9 182.0 %all-gather.10.cloned.1.call-start = ((), (), s32[]{:S(2)}) async-start(), calls=%async_computation.5 | async-start | bytes 5242880 | tf_op jit(solution)/shard_map/all_gather | solution.py:77
  8.7 193.2 %all-gather.8.cloned.1.call-start = ((), (), s32[]{:S(2)}) async-start(), calls=%async_computation.4 | async-start | bytes 5242880 | tf_op jit(solution)/shard_map/all_gather | solution.py:78
  9.4 289.8 %all-gather.12.cloned.1.call-start = ((), (), s32[]{:S(2)}) async-start(), calls=%async_computation.6 | async-start | bytes 10485760 | tf_op jit(solution)/shard_map/all_gather | solution.py:63
  9.4 71.3 %collective-permute-start.3 = (bf16[1,1,512,2048]{3,2,1,0:T(8,128)(2,1)}, bf16[1,1,512,2048]{3,2,1,0:T(8,128)(2,1)S(1)}, u32[]{:S(2)}, u32[]{:S(2)}) collective-permute-start(bf16[1,1,512,2048]{3,2,1,0:T(8,128)(2,1)} %param.13), channel_id=1, source_target_pairs={{0,16},{16,0},{1,17},{17,1},{2,18},{18,2},{3,19},{19,3},{4,20},{20... | collective-permute-start | bytes 6291464 | tf_op jit(solution)/shard_map/ppermute | solution.py:19
  82.2 322.5 %all-gather.14.cloned.1.call-start = ((), (), s32[]{:S(2)}) async-start(), calls=%async_computation.7 | async-start | bytes 20971520 | tf_op jit(solution)/shard_map/all_gather | solution.py:70
  82.8 61.1 %copy-start.15 = (s32[1,2]{1,0:T(1,128)S(1)}, s32[1,2]{1,0:T(1,128)}, u32[]{:S(2)}) copy-start(s32[1,2]{1,0:T(1,128)} %param.15) | copy-start | bytes 28
  82.8 455.0 %reduce-scatter.4.cloned.1.call-start = ((), (), s32[]{:S(2)}) async-start(), calls=%async_computation.8 | async-start | bytes 5242880 | tf_op jit(solution)/shard_map/reduce_scatter | solution.py:122
  86.6 26.2 %collective-permute-start = (bf16[256,2048]{1,0:T(8,128)(2,1)S(1)}, bf16[256,2048]{1,0:T(8,128)(2,1)S(1)}, u32[]{:S(2)}, u32[]{:S(2)}) collective-permute-start(bf16[256,2048]{1,0:T(8,128)(2,1)S(1)} %fusion.30), channel_id=1, source_target_pairs={{0,4},{4,8},{8,12},{12,0},{1,5},{5,9},{9,13},{13,1},{2,6},{6,10},{... | collective-permute-start | bytes 3145736 | tf_op jit(solution)/shard_map/ppermute | solution.py:94
  113.7 25.3 %collective-permute-start.1 = (bf16[256,2048]{1,0:T(8,128)(2,1)S(1)}, bf16[256,2048]{1,0:T(8,128)(2,1)}, u32[]{:S(2)}, u32[]{:S(2)}) collective-permute-start(bf16[256,2048]{1,0:T(8,128)(2,1)S(1)} %collective-permute-done), channel_id=1, source_target_pairs={{0,4},{4,8},{8,12},{12,0},{1,5},{5,9},{9,13},{13,1},{2,6},{6,10},{... | collective-permute-start | bytes 3145736 | tf_op jit(solution)/shard_map/ppermute | solution.py:94
  139.0 36.1 %collective-permute-start.2 = (bf16[256,2048]{1,0:T(8,128)(2,1)}, bf16[256,2048]{1,0:T(8,128)(2,1)}, u32[]{:S(2)}, u32[]{:S(2)}) collective-permute-start(bf16[256,2048]{1,0:T(8,128)(2,1)} %collective-permute-done.1), channel_id=1, source_target_pairs={{0,4},{4,8},{8,12},{12,0},{1,5},{5,9},{9,13},{13,1},{2,6},{6,10},{... | collective-permute-start | bytes 3145736 | tf_op jit(solution)/shard_map/ppermute | solution.py:94
  196.3 4.8 copy-start.12
  404.6 21.4 %copy-start.14 = (f32[1,8192]{1,0:T(1,128)S(1)}, f32[1,8192]{1,0:T(1,128)}, u32[]{:S(2)}) copy-start(f32[1,8192]{1,0:T(1,128)} %param.18) | copy-start | bytes 98308
  426.1 14.8 %copy-start.13 = (f32[1,128]{1,0:T(1,128)S(1)}, f32[1,128]{1,0:T(1,128)}, u32[]{:S(2)}) copy-start(f32[1,128]{1,0:T(1,128)} %param.22) | copy-start | bytes 1540
  447.2 3.9 copy-start.7
  447.2 4.7 copy-start.8
  447.2 4.7 copy-start.11
  447.2 4.7 copy-start.16
  460.9 151.9 %reduce-scatter.8.cloned.1.call-start = ((), (), s32[]{:S(2)}) async-start(), calls=%async_computation.10 | async-start | bytes 10485760 | tf_op jit(solution)/shard_map/reduce_scatter | solution.py:142
  460.9 5.6 copy-start.2
  477.5 170.0 %reduce-scatter.6.cloned.1.call-start = ((), (), s32[]{:S(2)}) async-start(), calls=%async_computation.9 | async-start | bytes 3145728 | tf_op jit(solution)/shard_map/reduce_scatter | solution.py:127
  544.6 3.7 copy-start.4
  549.4 98.1 %copy-start.1 = (s32[1,2]{1,0:T(1,128)S(1)}, s32[1,2]{1,0:T(1,128)}, u32[]{:S(2)}) copy-start(s32[1,2]{1,0:T(1,128)} %param.17) | copy-start | bytes 28
  (5 other events, 9.0 us)
Sparse Core Ops, SparseCore 0:
  9.6 58.3 all-gather.5
  69.6 34.4 all-gather.9
  105.6 34.4 all-gather.7
  141.6 157.5 all-gather.11
  300.6 104.0 all-gather.13
  461.0 76.7 reduce-scatter.3
  540.6 72.2 reduce-scatter.7
  615.6 31.8 reduce-scatter.5
